TPU v7x, 256 devices: a whole 4x4x8 slice. The times are simulated.
256 devices in a mesh: fsdp: 16 (over x, y), seq: 16 (over z, core).
Axes of the slice: x: 4, y: 4, z: 8, core: 2. Of those that a mesh axis runs over, the one named last changes fastest.
Arguments:
- tokens: bfloat16 [65536, 2048], P(('fsdp', 'seq')), may hold values from -6 to 6
- seq_lengths: int32 [16, 4], P('fsdp'), may hold values from 1 to 2048, 4096 in all within a row
- in_weight: bfloat16 [2048, 6144], P(None, 'fsdp'), may hold values from -0.125 to 0.125
- short_filter: float32 [7, 6144], replicated, may hold values from -2.5 to 2.5
- long_filter: bfloat16 [128, 128], replicated, may hold values from -0.5 to 0.5
- out_weight: bfloat16 [2048, 2048], replicated, may hold values from -0.125 to 0.125
Outputs:
- mixed: bfloat16 [65536, 2048], P(('fsdp', 'seq'))
Inputs may be any that keep to these rules, and one draw needn't show every extreme that they name: `seq_lengths`: in each pack the 4 lengths sum to 4096 and the longest is exactly 2048.
All inputs are finite; a program needn't handle non-finite values.
Results may differ from a plain program's by a relative error of at most 0.0073.
Values may be sent and summed in bfloat16 or wider, within the bound.
No kernel may reach another device: no remote copies, remote signals or barrier semaphores. Data moves between devices by JAX's collectives and lax.ppermute only.
A program may use at most 128 MiB of HBM per device.

v0:
```python
import jax
import jax.numpy as jnp
from jax import lax
from jax.sharding import PartitionSpec as P

LANE = 128
GROUP_DEVS = 4


def positions(row_ids, seq_starts):
    seq_begin = jnp.max(
        jnp.where(seq_starts[None, :] <= row_ids[:, None], seq_starts[None, :], 0), axis=1
    )
    return row_ids - seq_begin


def tap_table(tap_ids, long_filter):
    filter_len = long_filter.shape[0]
    one_hot = (
        tap_ids[:, :, None] == jnp.arange(filter_len, dtype=jnp.int32)[None, None, :]
    ).astype(jnp.bfloat16)
    return jnp.einsum(
        "ijt,tg->gij", one_hot, long_filter, preferred_element_type=jnp.float32
    ).astype(jnp.bfloat16)


def local(tokens, seq_lengths, in_weight, short_filter, long_filter, out_weight):
    rows, channels = tokens.shape
    width = short_filter.shape[0]
    filter_len, group_count = long_filter.shape
    per_group = channels // group_count
    n_seq = lax.axis_size("seq")
    s = lax.axis_index("seq")
    member = s % GROUP_DEVS
    part = LANE // GROUP_DEVS
    n_lblk = channels // LANE
    tail = filter_len + 8
    span = GROUP_DEVS * rows
    ext_rows = tail + span
    swaps = [[(i, i ^ d) for i in range(n_seq)] for d in range(1, GROUP_DEVS)]
    from_member = [tokens, lax.ppermute(tokens, "seq", swaps[0])]
    for d in range(2, GROUP_DEVS, 2):
        fetched = lax.ppermute(tokens, "seq", swaps[d - 1])
        from_member += [fetched, lax.ppermute(fetched, "seq", swaps[0])]
    blocks = []
    for m in range(GROUP_DEVS):
        pick = from_member[0]
        for d in range(1, GROUP_DEVS):
            pick = jnp.where(member ^ d == m, from_member[d], pick)
        blocks.append(pick)
    tail_src = tokens[rows - tail :]
    tail_tok = jnp.zeros_like(tail_src)
    for m in range(GROUP_DEVS):
        dist = m + 1
        perm = [(i - dist, i) for i in range(GROUP_DEVS, n_seq) if i % GROUP_DEVS == m]
        got = lax.ppermute(tail_src, "seq", perm)
        tail_tok = jnp.where(member == m, got, tail_tok)
    ext_tokens = jnp.concatenate([tail_tok] + blocks, axis=0)
    lengths_row = seq_lengths[0]
    seq_starts = jnp.cumsum(lengths_row) - lengths_row
    pair_start = s // GROUP_DEVS * span
    row_ids = pair_start - tail + jnp.arange(ext_rows, dtype=jnp.int32)
    position = positions(row_ids, seq_starts)
    offset = member * part
    w_t = in_weight.T.reshape(in_weight.shape[1] // LANE, LANE, channels)
    w_part = lax.dynamic_slice_in_dim(w_t, offset, part, axis=1)
    w_all = lax.all_gather(w_part, "fsdp", axis=0, tiled=True)
    own = n_lblk * part
    w_all = w_all.reshape(3 * own, channels)
    ow = out_weight.reshape(n_lblk, LANE, channels)
    weights = []
    for d in range(GROUP_DEVS):
        src_offset = (member ^ d) * part
        weights.append(
            lax.dynamic_slice_in_dim(ow, src_offset, part, axis=1).reshape(own, channels)
        )
    ow_cat = jnp.concatenate(weights, axis=0)
    ext_tokens, ow_cat = lax.optimization_barrier((ext_tokens, ow_cat))
    projected = jnp.dot(ext_tokens, w_all.T, preferred_element_type=jnp.float32).astype(
        jnp.bfloat16
    )
    taps = short_filter.reshape(width, 3, n_lblk, LANE)
    taps = lax.dynamic_slice_in_dim(taps, offset, part, axis=3).reshape(width, 3 * own)
    start = 8
    feat_rows = ext_rows - start
    pos_f = position[start:]
    featured = jnp.zeros((feat_rows, 3 * own), jnp.float32)
    for tap_index in range(width):
        shifted = projected[start - tap_index : ext_rows - tap_index].astype(jnp.float32)
        featured = featured + taps[tap_index] * jnp.where(
            (pos_f >= tap_index)[:, None], shifted, 0.0
        )
    queries = featured[feat_rows - span :, :own]
    mixed_in = (featured[:, own : 2 * own] * featured[:, 2 * own :]).astype(jnp.bfloat16)
    sub = LANE // per_group
    lf = long_filter.reshape(filter_len, n_lblk, sub)
    lf = lax.dynamic_slice_in_dim(lf, offset // per_group, part // per_group, axis=2)
    lf = lf.reshape(filter_len, own // per_group)
    n_groups = own // per_group
    out_rows = jnp.arange(filter_len, dtype=jnp.int32)[:, None]
    src_rows = jnp.arange(filter_len, dtype=jnp.int32)[None, :]
    cur_tap = out_rows - src_rows
    prev_tap = out_rows + filter_len - src_rows
    cur_table = tap_table(cur_tap, lf)
    prev_table = tap_table(prev_tap, lf)
    n_blocks = span // filter_len
    pos_out = position[tail:].reshape(n_blocks, filter_len)
    cur_kernel = jnp.where(
        (cur_tap[None] <= pos_out[:, :, None])[:, None], cur_table[None], 0.0
    ).astype(jnp.bfloat16)
    prev_kernel = jnp.where(
        (prev_tap[None] <= pos_out[:, :, None])[:, None], prev_table[None], 0.0
    ).astype(jnp.bfloat16)
    mi_t = mixed_in.T.reshape(n_groups, per_group, n_blocks + 1, filter_len)
    filtered = jnp.einsum(
        "gcbj,bgij->gcbi", mi_t[:, :, 1:], cur_kernel, preferred_element_type=jnp.float32
    )
    filtered = filtered + jnp.einsum(
        "gcbj,bgij->gcbi", mi_t[:, :, :-1], prev_kernel, preferred_element_type=jnp.float32
    )
    filtered = filtered.reshape(own, span)
    gated = (queries.T * filtered).astype(jnp.bfloat16)
    gated = gated.T.reshape(GROUP_DEVS, rows, own)
    pieces = []
    for d in range(GROUP_DEVS):
        send = lax.dynamic_index_in_dim(gated, member ^ d, axis=0, keepdims=False)
        got = send if d == 0 else lax.ppermute(send, "seq", swaps[d - 1])
        pieces.append(got)
    result = tokens.astype(jnp.float32) + jnp.dot(
        jnp.concatenate(pieces, axis=1), ow_cat, preferred_element_type=jnp.float32
    )
    return result.astype(jnp.bfloat16)


def solution(mesh):
    in_specs = (P(("fsdp", "seq"), None), P("fsdp", None), P(None, "fsdp"), P(), P(), P())
    out_specs = P(("fsdp", "seq"), None)
    return jax.shard_map(local, mesh=mesh, in_specs=in_specs, out_specs=out_specs, check_vma=False)
```

profile of v0, /device:TPU:1, one launch (start us, length us, event | category | flops | bytes accessed | tf_op | source)
XLA Modules:
  0.0 154.7 jit_solution(10799367417863991124)
XLA Ops:
  6.5 1.8 %copy.26 = bf16[2048,384]{0,1:T(8,128)(2,1)S(1)} copy(bf16[2048,384]{1,0:T(8,128)(2,1)} %param.8) | data formatting | bytes 3145728 | tf_op args[2]
  15.4 8.6 %collective-permute-start.4 = (bf16[256,2048]{1,0:T(8,128)(2,1)S(1)}, bf16[256,2048]{1,0:T(8,128)(2,1)S(1)}, u32[]{:S(2)}, u32[]{:S(2)}) collective-permute-start(bf16[256,2048]{1,0:T(8,128)(2,1)S(1)} %copy-done.1), channel_id=1, source_target_pairs={{0,2},{1,3},{2,0},{3,1},{4,6},{5,7},{6,4},{7,5},{8,10},{9,11},{10,... | collective-permute-start | bytes 3145736 | tf_op jit(solution)/shard_map/ppermute | solution.py:43
  27.4 4.0 %fusion.20 = bf16[32,128,128]{2,0,1:T(8,128)(2,1)S(1)} fusion(bf16[128,32,1]{0,1,2:T(8,128)(2,1)S(1)} %bitcast.77, s32[128,128]{1,0:T(8,128)S(1)} %get-tuple-element.35), kind=kOutput, calls=%fused_computation.28 | convolution fusion | flops 136839168 | bytes 1122304 | tf_op jit(solution)/shard_map/ijt,tg->gij/dot_general | solution.py:22
  32.8 3.9 %fusion.21 = bf16[32,128,128]{2,0,1:T(8,128)(2,1)S(1)} fusion(bf16[128,32,1]{0,1,2:T(8,128)(2,1)S(1)} %bitcast.78, s32[128,128]{1,0:T(8,128)S(1)} %get-tuple-element.36), kind=kOutput, calls=%fused_computation.29 | convolution fusion | flops 136839168 | bytes 1122304 | tf_op jit(solution)/shard_map/ijt,tg->gij/dot_general | solution.py:22
  39.2 4.3 %constant_dynamic-slice_fusion.11 = (bf16[16,32,2048]{2,1,0:T(8,128)(2,1)S(1)}, bf16[16,32,2048]{2,1,0:T(8,128)(2,1)S(1)}, bf16[16,32,2048]{2,1,0:T(8,128)(2,1)S(1)}, bf16[16,32,2048]{2,1,0:T(8,128)(2,1)S(1)}) fusion(bf16[16,128,2048]{2,1,0:T(8,128)(2,1)} %bitcast.65, s32[]{:T(128)S(6)} %select_n.178, s32[]{:T(128)S(6)} %select_n.215, s32[]{:T(128)S(6)} %select_n.214, ...), kind=kLoop, calls=%fused_computation.73 | loop fusion | bytes 16777232 | tf_op jit(solution)/shard_map/dynamic_slice | solution.py:75
  44.2 4.1 %pad_maximum_fusion = bf16[2048,2048]{1,0:T(8,128)(2,1)} fusion(bf16[512,2048]{1,0:T(8,128)(2,1)S(1)} %bitcast.69, bf16[512,2048]{1,0:T(8,128)(2,1)S(1)} %bitcast.70, bf16[512,2048]{1,0:T(8,128)(2,1)S(1)} %bitcast.71, bf16[512,2048]{1,0:T(8,128)(2,1)S(1)} %bitcast.68), kind=kLoop, calls=%fused_computation | loop fusion | flops 33554432 | bytes 16777216 | tf_op jit(solution)/shard_map/concatenate | solution.py:77
  48.3 2.3 %select_dynamic-update-slice_fusion.4 = bf16[1160,2048]{1,0:T(8,128)(2,1)} fusion(bf16[136,2048]{1,0:T(8,128)(2,1)S(1)} %collective-permute-done, bf16[136,2048]{1,0:T(8,128)(2,1)} %collective-permute-done.1, bf16[136,2048]{1,0:T(8,128)(2,1)} %collective-permute-done.2, bf16[136,2048]{1,0:T(8,128)(2,1)} %collective-permute-done.3, pred[]{:T(512)S(6)} %eq.79, ...), kind=kLoop, calls=%fused_computation.44 | loop fusion | flops 1114111 | bytes 2785284
  50.6 1.7 %select_dynamic-update-slice_fusion.3 = bf16[1160,2048]{1,0:T(8,128)(2,1)} fusion(bf16[1160,2048]{1,0:T(8,128)(2,1)} %select_dynamic-update-slice_fusion.4, bf16[256,2048]{1,0:T(8,128)(2,1)S(1)} %collective-permute-done.5, bf16[256,2048]{1,0:T(8,128)(2,1)S(1)} %collective-permute-done.4, bf16[256,2048]{1,0:T(8,128)(2,1)S(1)} %collective-permute-done.6, ...), kind=kLoop, calls=%fused_computation.43 | loop fusion | flops 1572864 | bytes 5242883
  52.3 1.7 %select_dynamic-update-slice_fusion.2 = bf16[1160,2048]{1,0:T(8,128)(2,1)} fusion(bf16[1160,2048]{1,0:T(8,128)(2,1)} %select_dynamic-update-slice_fusion.3, bf16[256,2048]{1,0:T(8,128)(2,1)S(1)} %collective-permute-done.5, bf16[256,2048]{1,0:T(8,128)(2,1)S(1)} %collective-permute-done.4, bf16[256,2048]{1,0:T(8,128)(2,1)S(1)} %collective-permute-done.6, ...), kind=kLoop, calls=%fused_computation.42 | loop fusion | flops 1572864 | bytes 5242883
  54.0 1.7 %select_dynamic-update-slice_fusion.1 = bf16[1160,2048]{1,0:T(8,128)(2,1)} fusion(bf16[1160,2048]{1,0:T(8,128)(2,1)} %select_dynamic-update-slice_fusion.2, bf16[256,2048]{1,0:T(8,128)(2,1)S(1)} %collective-permute-done.5, bf16[256,2048]{1,0:T(8,128)(2,1)S(1)} %collective-permute-done.4, bf16[256,2048]{1,0:T(8,128)(2,1)S(1)} %collective-permute-done.6, ...), kind=kLoop, calls=%fused_computation.41 | loop fusion | flops 1572864 | bytes 5242883
  55.7 1.7 %select_dynamic-update-slice_fusion = bf16[1160,2048]{1,0:T(8,128)(2,1)} fusion(bf16[1160,2048]{1,0:T(8,128)(2,1)} %select_dynamic-update-slice_fusion.1, bf16[256,2048]{1,0:T(8,128)(2,1)S(1)} %collective-permute-done.5, bf16[256,2048]{1,0:T(8,128)(2,1)S(1)} %collective-permute-done.4, bf16[256,2048]{1,0:T(8,128)(2,1)S(1)} %collective-permute-done.6, ...), kind=kLoop, calls=%fused_computation.40 | loop fusion | flops 1572864 | bytes 5242883 | tf_op jit(solution)/shard_map/concatenate | solution.py:58
  57.4 22.7 %all-gather.2.cloned.1.call-done = bf16[48,32,2048]{2,1,0:T(8,128)(2,1)} async-done(((bf16[3,32,2048]{2,1,0:T(8,128)(2,1)}), bf16[48,32,2048]{2,1,0:T(8,128)(2,1)}) %all-gather.2.cloned.1.call-update) | async-done | bytes 6291472 | tf_op jit(solution)/shard_map/all_gather | solution.py:67
  80.1 11.2 %convolution_convert_fusion = bf16[1160,1536]{1,0:T(8,128)(2,1)S(1)} fusion(bf16[1160,2048]{1,0:T(8,128)(2,1)} %select_dynamic-update-slice_fusion, bf16[1536,2048]{1,0:T(8,128)(2,1)} %bitcast.79), kind=kOutput, calls=%fused_computation.11 | convolution fusion | flops 7299870720 | bytes 14606336 | tf_op jit(solution)/shard_map/dot_general | solution.py:79
  91.2 10.7 %multiply_add_fusion = f32[1152,1536]{1,0:T(8,128)S(1)} fusion(bf16[1160,1536]{1,0:T(8,128)(2,1)S(1)} %convolution_convert_fusion, f32[1536]{0:T(1024)S(1)} %mul.115, f32[1536]{0:T(1024)S(1)} %mul.112, f32[1536]{0:T(1024)S(1)} %mul.109, f32[1536]{0:T(1024)S(1)} %mul.106, f32[1536]{0:T(1024)S(1)} %mul.103, f32[1536]{0:T(1024)S(1)} %mul.100, ...), kind=kLoop, calls=%fused_computation.12 | loop fusion | flops 47775744 | bytes 31901568 | tf_op jit(solution)/shard_map/add | solution.py:90
  101.9 2.9 %copy-done = f32[1152,1536]{1,0:T(8,128)} copy-done((f32[1152,1536]{1,0:T(8,128)}, f32[1152,1536]{1,0:T(8,128)S(1)}, u32[]{:S(2)}) %copy-start) | copy-done | bytes 7077912
  106.7 2.7 %reshape.154 = bf16[32,16,9,128]{3,2,1,0:T(8,128)(2,1)S(1)} reshape(bf16[512,1152]{1,0:T(8,128)(2,1)} %copy.29) | data formatting | bytes 2359296 | tf_op jit(solution)/shard_map/reshape | solution.py:114
  109.9 5.8 %fusion = f32[32,8,128,16]{2,3,1,0:T(8,128)S(1)} fusion(pred[8,128,128]{2,1,0:T(8,128)(4,1)S(1)} %copy-done.3, bf16[32,128,128]{2,1,0:T(8,128)(2,1)} %copy.31, bf16[32,16,8,128]{3,2,1,0:T(8,128)(2,1)S(1)} %get-tuple-element.14), kind=kOutput, calls=%fused_computation.1 | convolution fusion | flops 138412032 | bytes 4325376 | tf_op jit(solution)/shard_map/gcbj,bgij->gcbi/dot_general | solution.py:118
  115.6 4.5 %add_bitcast_fusion = f32[32,16,8,128]{3,1,2,0:T(8,128)S(1)} fusion(f32[32,8,128,16]{2,3,1,0:T(8,128)S(1)} %fusion, pred[8,128,128]{2,1,0:T(8,128)(4,1)S(1)} %get-tuple-element.33, bf16[32,128,128]{2,1,0:T(8,128)(2,1)S(1)} %copy-done.2, bf16[32,16,8,128]{3,2,1,0:T(8,128)(2,1)S(1)} %get-tuple-element.13), kind=kOutput, calls=%fused_computation.27 | convolution fusion | flops 138936320 | bytes 6422528 | tf_op jit(solution)/shard_map/gcbj,bgij->gcbi/dot_general | solution.py:115
  121.0 1.8 %copy.44 = f32[64,8,8,128]{3,1,2,0:T(8,128)} copy(f32[64,8,8,128]{3,2,1,0:T(8,128)S(1)} %bitcast.66) | data formatting | bytes 4194304
  122.8 1.9 %copy.34 = f32[512,1024]{0,1:T(8,128)S(1)} copy(f32[512,1024]{1,0:T(8,128)} %bitcast.67) | data formatting | bytes 4194304 | tf_op jit(solution)/shard_map/reshape | solution.py:121
  124.7 1.9 %fusion.17 = bf16[512,1024]{0,1:T(8,128)(2,1)S(1)} fusion(f32[512,1024]{0,1:T(8,128)S(1)} %copy.34, f32[1152,1536]{1,0:T(8,128)} %copy-done), kind=kLoop, calls=%fused_computation.26 | loop fusion | flops 1048576 | bytes 5242880 | tf_op jit(solution)/shard_map/convert_element_type | solution.py:122
  129.2 6.1 %collective-permute-done.8 = bf16[256,512]{1,0:T(8,128)(2,1)S(1)} collective-permute-done((bf16[256,512]{1,0:T(8,128)(2,1)S(1)}, bf16[256,512]{1,0:T(8,128)(2,1)S(1)}, u32[]{:S(2)}, u32[]{:S(2)}) %collective-permute-start.8) | collective-permute-done | bytes 262176 | tf_op jit(solution)/shard_map/ppermute | solution.py:127
  135.4 5.8 %collective-permute-done.9 = bf16[256,512]{1,0:T(8,128)(2,1)S(1)} collective-permute-done((bf16[256,512]{1,0:T(8,128)(2,1)S(1)}, bf16[256,512]{1,0:T(8,128)(2,1)S(1)}, u32[]{:S(2)}, u32[]{:S(2)}) %collective-permute-start.9) | collective-permute-done | bytes 262176 | tf_op jit(solution)/shard_map/ppermute | solution.py:127
  141.2 6.7 %fusion.14 = bf16[256,2048]{1,0:T(8,128)(2,1)} fusion(bf16[2048,2048]{1,0:T(8,128)(2,1)} %pad_maximum_fusion, bf16[256,2048]{1,0:T(8,128)(2,1)S(1)} %copy-done.1, bf16[256,512]{1,0:T(8,128)(2,1)S(1)} %collective-permute-done.9, bf16[256,512]{1,0:T(8,128)(2,1)S(1)} %collective-permute-done.8, bf16[256,512]{1,0:T(8,128)(2,1)S(1)} %collective-permute-done.7, ...), kind=kOutput, calls=%fused_computation.20 | convolution fusion | flops 2153250816 | bytes 11534336 | tf_op jit(solution)/shard_map/dot_general | solution.py:129
  (58 shorter events, 20.6 us)
Async XLA Ops:
  6.5 8.8 %copy-start.1 = (bf16[256,2048]{1,0:T(8,128)(2,1)S(1)}, bf16[256,2048]{1,0:T(8,128)(2,1)}, u32[]{:S(2)}) copy-start(bf16[256,2048]{1,0:T(8,128)(2,1)} %param.6) | copy-start | bytes 3145732
  6.5 73.5 %all-gather.2.cloned.1.call-start = ((), (), s32[]{:S(2)}) async-start(), calls=%async_computation | async-start | bytes 6684672 | tf_op jit(solution)/shard_map/all_gather | solution.py:67
  10.3 33.3 %collective-permute-start = (bf16[136,2048]{1,0:T(8,128)(2,1)S(1)}, bf16[136,2048]{1,0:T(8,128)(2,1)S(1)}, u32[]{:S(2)}, u32[]{:S(2)}) collective-permute-start(bf16[136,2048]{1,0:T(8,128)(2,1)S(1)} %slice.75), channel_id=1, source_target_pairs={{3,7},{7,11},{11,15},{19,23},{23,27},{27,31},{35,39},{39,43},{43,4... | collective-permute-start | bytes 1671176 | tf_op jit(solution)/shard_map/ppermute | solution.py:56
  11.0 37.3 %collective-permute-start.1 = (bf16[136,2048]{1,0:T(8,128)(2,1)S(1)}, bf16[136,2048]{1,0:T(8,128)(2,1)}, u32[]{:S(2)}, u32[]{:S(2)}) collective-permute-start(bf16[136,2048]{1,0:T(8,128)(2,1)S(1)} %slice.75), channel_id=1, source_target_pairs={{3,6},{7,10},{11,14},{19,22},{23,26},{27,30},{35,38},{39,42},{43,4... | collective-permute-start | bytes 1671176 | tf_op jit(solution)/shard_map/ppermute | solution.py:56
  12.4 35.8 %collective-permute-start.2 = (bf16[136,2048]{1,0:T(8,128)(2,1)S(1)}, bf16[136,2048]{1,0:T(8,128)(2,1)}, u32[]{:S(2)}, u32[]{:S(2)}) collective-permute-start(bf16[136,2048]{1,0:T(8,128)(2,1)S(1)} %slice.75), channel_id=1, source_target_pairs={{3,5},{7,9},{11,13},{19,21},{23,25},{27,29},{35,37},{39,41},{43,45... | collective-permute-start | bytes 1671176 | tf_op jit(solution)/shard_map/ppermute | solution.py:56
  13.9 34.4 %collective-permute-start.3 = (bf16[136,2048]{1,0:T(8,128)(2,1)S(1)}, bf16[136,2048]{1,0:T(8,128)(2,1)}, u32[]{:S(2)}, u32[]{:S(2)}) collective-permute-start(bf16[136,2048]{1,0:T(8,128)(2,1)S(1)} %slice.75), channel_id=1, source_target_pairs={{3,4},{7,8},{11,12},{19,20},{23,24},{27,28},{35,36},{39,40},{43,44... | collective-permute-start | bytes 1671176 | tf_op jit(solution)/shard_map/ppermute | solution.py:56
  15.4 28.6 %collective-permute-start.4 = (bf16[256,2048]{1,0:T(8,128)(2,1)S(1)}, bf16[256,2048]{1,0:T(8,128)(2,1)S(1)}, u32[]{:S(2)}, u32[]{:S(2)}) collective-permute-start(bf16[256,2048]{1,0:T(8,128)(2,1)S(1)} %copy-done.1), channel_id=1, source_target_pairs={{0,2},{1,3},{2,0},{3,1},{4,6},{5,7},{6,4},{7,5},{8,10},{9,11},{10,... | collective-permute-start | bytes 3145736 | tf_op jit(solution)/shard_map/ppermute | solution.py:43
  25.5 12.6 %copy-start.4 = (s32[1,4]{1,0:T(1,128)S(1)}, s32[1,4]{1,0:T(1,128)}, u32[]{:S(2)}) copy-start(s32[1,4]{1,0:T(1,128)} %param.7) | copy-start | bytes 52
  43.6 7.0 %collective-permute-start.6 = (bf16[256,2048]{1,0:T(8,128)(2,1)S(1)}, bf16[256,2048]{1,0:T(8,128)(2,1)S(1)}, u32[]{:S(2)}, u32[]{:S(2)}) collective-permute-start(bf16[256,2048]{1,0:T(8,128)(2,1)S(1)} %copy-done.1), channel_id=1, source_target_pairs={{0,1},{1,0},{2,3},{3,2},{4,5},{5,4},{6,7},{7,6},{8,9},{9,8},{10,11... | collective-permute-start | bytes 3145736 | tf_op jit(solution)/shard_map/ppermute | solution.py:41
  44.0 6.6 %collective-permute-start.5 = (bf16[256,2048]{1,0:T(8,128)(2,1)S(1)}, bf16[256,2048]{1,0:T(8,128)(2,1)S(1)}, u32[]{:S(2)}, u32[]{:S(2)}) collective-permute-start(bf16[256,2048]{1,0:T(8,128)(2,1)S(1)} %collective-permute-done.4), channel_id=1, source_target_pairs={{0,1},{1,0},{2,3},{3,2},{4,5},{5,4},{6,7},{7,6},{8,9},{9,8},{10,11... | collective-permute-start | bytes 3145736 | tf_op jit(solution)/shard_map/ppermute | solution.py:44
  101.9 2.9 %copy-start = (f32[1152,1536]{1,0:T(8,128)}, f32[1152,1536]{1,0:T(8,128)S(1)}, u32[]{:S(2)}) copy-start(f32[1152,1536]{1,0:T(8,128)S(1)} %multiply_add_fusion) | copy-start | bytes 21233668
  105.3 4.6 %copy-start.3 = (pred[8,128,128]{2,1,0:T(8,128)(4,1)S(1)}, pred[8,128,128]{2,1,0:T(8,128)(4,1)}, u32[]{:S(2)}) copy-start(pred[8,128,128]{2,1,0:T(8,128)(4,1)} %get-tuple-element.34) | copy-start | bytes 393220
  109.9 5.8 %copy-start.2 = (bf16[32,128,128]{2,1,0:T(8,128)(2,1)S(1)}, bf16[32,128,128]{2,1,0:T(8,128)(2,1)}, u32[]{:S(2)}) copy-start(bf16[32,128,128]{2,1,0:T(8,128)(2,1)} %copy.28) | copy-start | bytes 3145732
  126.7 2.5 %collective-permute-start.7 = (bf16[256,512]{1,0:T(8,128)(2,1)S(1)}, bf16[256,512]{1,0:T(8,128)(2,1)S(1)}, u32[]{:S(2)}, u32[]{:S(2)}) collective-permute-start(bf16[256,512]{1,0:T(8,128)(2,1)S(1)} %get-tuple-element.18), channel_id=1, source_target_pairs={{0,1},{1,0},{2,3},{3,2},{4,5},{5,4},{6,7},{7,6},{8,9},{9,8},{10,11... | collective-permute-start | bytes 786440 | tf_op jit(solution)/shard_map/ppermute | solution.py:127
  127.5 7.9 %collective-permute-start.8 = (bf16[256,512]{1,0:T(8,128)(2,1)S(1)}, bf16[256,512]{1,0:T(8,128)(2,1)S(1)}, u32[]{:S(2)}, u32[]{:S(2)}) collective-permute-start(bf16[256,512]{1,0:T(8,128)(2,1)S(1)} %get-tuple-element.17), channel_id=1, source_target_pairs={{0,2},{1,3},{2,0},{3,1},{4,6},{5,7},{6,4},{7,5},{8,10},{9,11},{10,... | collective-permute-start | bytes 786440 | tf_op jit(solution)/shard_map/ppermute | solution.py:127
  128.8 12.4 %collective-permute-start.9 = (bf16[256,512]{1,0:T(8,128)(2,1)S(1)}, bf16[256,512]{1,0:T(8,128)(2,1)S(1)}, u32[]{:S(2)}, u32[]{:S(2)}) collective-permute-start(bf16[256,512]{1,0:T(8,128)(2,1)S(1)} %get-tuple-element.16), channel_id=1, source_target_pairs={{0,3},{1,2},{2,1},{3,0},{4,7},{5,6},{6,5},{7,4},{8,11},{9,10},{10,... | collective-permute-start | bytes 786440 | tf_op jit(solution)/shard_map/ppermute | solution.py:127
Sparse Core Ops, SparseCore 0:
  9.8 70.1 all-gather.1
where the time goes:
time: 155 us
  matrix products  36 us (23%)
  waiting for transfers between devices  34.9 us (23%)
  other arithmetic  28.2 us (18%)
  local copies, waits for them, and re-layouts  25.5 us (16%)
  starting transfers between devices  16.5 us (11%)
  between operations  13.6 us (9%)
    all_gather x1, waiting for transfers between devices, local(): w_all = lax.all_gather(w_part, 'fsdp', axis=0, tiled=True)  22.7 us
    ppermute x3, waiting for transfers between devices, local(): got = send if d == 0 else lax.ppermute(send, 'seq', swaps[d - 1])  11.9 us
    dot_general x1, matrix products, local(): jnp.dot(ext_tokens, w_all.T, preferred_element_type=jnp.float32)  11.2 us
    add x1, other arithmetic, local(): featured + taps[tap_index] * jnp.where((pos_f >= tap_index)[:, None], shi...  10.7 us
    ppermute x1, starting transfers between devices, local(): fetched = lax.ppermute(tokens, 'seq', swaps[d - 1])  8.59 us
    unnamed x14, local copies, waits for them, and re-layouts  8.3 us
    dot_general x2, matrix products, tap_table(): jnp.einsum('ijt,tg->gij', one_hot, long_filter, preferred_element_type=jn...  7.92 us
    unnamed x4, other arithmetic  7.39 us
  transfers between devices with their start and end apart: 11, of which 4 were waited for; matrix products, arithmetic and copies ran while one was open for 22% of the time, Pallas kernels for 0%

commit v1 on v0

--- a/solution.py
+++ b/solution.py
@@ -64,7 +64,9 @@
     offset = member * part
     w_t = in_weight.T.reshape(in_weight.shape[1] // LANE, LANE, channels)
     w_part = lax.dynamic_slice_in_dim(w_t, offset, part, axis=1)
-    w_all = lax.all_gather(w_part, "fsdp", axis=0, tiled=True)
+    w_all = jnp.concatenate(
+        lax.all_to_all(jnp.stack([w_part] * lax.axis_size("fsdp")), "fsdp", 0, 0), axis=0
+    )
     own = n_lblk * part
     w_all = w_all.reshape(3 * own, channels)
     ow = out_weight.reshape(n_lblk, LANE, channels)

time: 155 us -> 204 us (1.32)
  the two profiles are of different devices: /device:TPU:1 before, /device:TPU:221 now
where the time goes in v1:
time: 204 us; the launch traced here: 203 us
  waiting for transfers between devices  91.9 us (45%)
  matrix products  36 us (18%)
  local copies, waits for them, and re-layouts  29.2 us (14%)
  other arithmetic  28.5 us (14%)
  starting transfers between devices  17.5 us (9%)
    all_to_all x1, waiting for transfers between devices, local(): lax.all_to_all(jnp.stack([w_part] * lax.axis_size('fsdp')), 'fsdp', 0, 0)  77.1 us
    ppermute x3, waiting for transfers between devices, local(): got = send if d == 0 else lax.ppermute(send, 'seq', swaps[d - 1])  11.9 us
    dot_general x1, matrix products, local(): jnp.dot(ext_tokens, w_all.T, preferred_element_type=jnp.float32)  11.2 us
    add x1, other arithmetic, local(): featured + taps[tap_index] * jnp.where((pos_f >= tap_index)[:, None], shi...  10.7 us
    dot_general x2, matrix products, tap_table(): jnp.einsum('ijt,tg->gij', one_hot, long_filter, preferred_element_type=jn...  7.91 us
    unnamed x4, other arithmetic  7.36 us
    all_to_all x1, starting transfers between devices, local(): lax.all_to_all(jnp.stack([w_part] * lax.axis_size('fsdp')), 'fsdp', 0, 0)  6.68 us
    dot_general x1, matrix products, local(): jnp.dot(jnp.concatenate(pieces, axis=1), ow_cat, preferred_element_type=j...  6.68 us
  transfers between devices with their start and end apart: 11, of which 4 were waited for; matrix products, arithmetic and copies ran while one was open for 17% of the time, Pallas kernels for 0%

profile of v1, /device:TPU:221, one launch (start us, length us, event | category | flops | bytes accessed | tf_op | source)
XLA Modules:
  0.0 203.5 jit_solution(12377657766877101748)
XLA Ops:
  0.0 1.9 slice.75
  10.1 3.4 %stack.2 = bf16[16,3,32,2048]{3,2,1,0:T(8,128)(2,1)} broadcast(bf16[3,32,2048]{2,1,0:T(8,128)(2,1)S(1)} %constant_dynamic-slice_fusion.7), dimensions={1,2,3} | broadcast | bytes 6684672 | tf_op jit(solution)/shard_map/stack | solution.py:68
  13.5 6.7 %all-to-all-start = ((bf16[16,3,32,2048]{3,2,1,0:T(8,128)(2,1)}), bf16[16,3,32,2048]{3,2,1,0:T(8,128)(2,1)}, u32[]{:S(2)}, u32[]{:S(2)}) async-start(bf16[16,3,32,2048]{3,2,1,0:T(8,128)(2,1)} %stack.2), calls=%async_computation | async-start | bytes 12582912 | tf_op jit(solution)/shard_map/all_to_all | solution.py:68
  21.3 4.0 %fusion.20 = bf16[32,128,128]{2,0,1:T(8,128)(2,1)S(1)} fusion(bf16[128,32,1]{0,1,2:T(8,128)(2,1)S(1)} %bitcast.77, s32[128,128]{1,0:T(8,128)S(1)} %get-tuple-element.35), kind=kOutput, calls=%fused_computation.28 | convolution fusion | flops 136839168 | bytes 1122304 | tf_op jit(solution)/shard_map/ijt,tg->gij/dot_general | solution.py:22
  26.7 3.9 %fusion.21 = bf16[32,128,128]{2,0,1:T(8,128)(2,1)S(1)} fusion(bf16[128,32,1]{0,1,2:T(8,128)(2,1)S(1)} %bitcast.78, s32[128,128]{1,0:T(8,128)S(1)} %get-tuple-element.36), kind=kOutput, calls=%fused_computation.29 | convolution fusion | flops 136839168 | bytes 1122304 | tf_op jit(solution)/shard_map/ijt,tg->gij/dot_general | solution.py:22
  32.5 4.4 %constant_dynamic-slice_fusion.11 = (bf16[16,32,2048]{2,1,0:T(8,128)(2,1)S(1)}, bf16[16,32,2048]{2,1,0:T(8,128)(2,1)S(1)}, bf16[16,32,2048]{2,1,0:T(8,128)(2,1)S(1)}, bf16[16,32,2048]{2,1,0:T(8,128)(2,1)S(1)}) fusion(bf16[16,128,2048]{2,1,0:T(8,128)(2,1)} %bitcast.65, s32[]{:T(128)S(6)} %select_n.178, s32[]{:T(128)S(6)} %select_n.215, s32[]{:T(128)S(6)} %select_n.214, ...), kind=kLoop, calls=%fused_computation.73 | loop fusion | bytes 16777232 | tf_op jit(solution)/shard_map/dynamic_slice | solution.py:77
  37.8 2.8 %collective-permute-done.4 = bf16[256,2048]{1,0:T(8,128)(2,1)S(1)} collective-permute-done((bf16[256,2048]{1,0:T(8,128)(2,1)}, bf16[256,2048]{1,0:T(8,128)(2,1)S(1)}, u32[]{:S(2)}, u32[]{:S(2)}) %collective-permute-start.4) | collective-permute-done | bytes 1048608 | tf_op jit(solution)/shard_map/ppermute | solution.py:43
  41.1 4.1 %pad_maximum_fusion = bf16[2048,2048]{1,0:T(8,128)(2,1)} fusion(bf16[512,2048]{1,0:T(8,128)(2,1)S(1)} %bitcast.69, bf16[512,2048]{1,0:T(8,128)(2,1)S(1)} %bitcast.70, bf16[512,2048]{1,0:T(8,128)(2,1)S(1)} %bitcast.71, bf16[512,2048]{1,0:T(8,128)(2,1)S(1)} %bitcast.68), kind=kLoop, calls=%fused_computation | loop fusion | flops 33554432 | bytes 16777216 | tf_op jit(solution)/shard_map/concatenate | solution.py:79
  45.2 2.3 %select_dynamic-update-slice_fusion.4 = bf16[1160,2048]{1,0:T(8,128)(2,1)} fusion(bf16[136,2048]{1,0:T(8,128)(2,1)S(1)} %collective-permute-done, bf16[136,2048]{1,0:T(8,128)(2,1)} %collective-permute-done.1, bf16[136,2048]{1,0:T(8,128)(2,1)} %collective-permute-done.2, bf16[136,2048]{1,0:T(8,128)(2,1)} %collective-permute-done.3, pred[]{:T(512)S(6)} %eq.79, ...), kind=kLoop, calls=%fused_computation.44 | loop fusion | flops 1114111 | bytes 2785284
  52.5 1.7 select_dynamic-update-slice_fusion
  54.3 77.1 %all-to-all-done = bf16[16,3,32,2048]{3,2,1,0:T(8,128)(2,1)} async-done(((bf16[16,3,32,2048]{3,2,1,0:T(8,128)(2,1)}), bf16[16,3,32,2048]{3,2,1,0:T(8,128)(2,1)}, u32[]{:S(2)}, u32[]{:S(2)}) %all-to-all-start) | async-done | bytes 6291488 | tf_op jit(solution)/shard_map/all_to_all | solution.py:68
  131.4 11.2 %convolution_convert_fusion = bf16[1160,1536]{1,0:T(8,128)(2,1)S(1)} fusion(bf16[1160,2048]{1,0:T(8,128)(2,1)} %select_dynamic-update-slice_fusion, bf16[1536,2048]{1,0:T(8,128)(2,1)} %bitcast.8), kind=kOutput, calls=%fused_computation.11 | convolution fusion | flops 7299870720 | bytes 14606336 | tf_op jit(solution)/shard_map/dot_general | solution.py:81
  142.5 10.7 %multiply_add_fusion = f32[1152,1536]{1,0:T(8,128)S(1)} fusion(bf16[1160,1536]{1,0:T(8,128)(2,1)S(1)} %convolution_convert_fusion, f32[1536]{0:T(1024)S(1)} %mul.115, f32[1536]{0:T(1024)S(1)} %mul.112, f32[1536]{0:T(1024)S(1)} %mul.109, f32[1536]{0:T(1024)S(1)} %mul.106, f32[1536]{0:T(1024)S(1)} %mul.103, f32[1536]{0:T(1024)S(1)} %mul.100, ...), kind=kLoop, calls=%fused_computation.12 | loop fusion | flops 47775744 | bytes 31901568 | tf_op jit(solution)/shard_map/add | solution.py:92
  153.2 2.9 %copy-done = f32[1152,1536]{1,0:T(8,128)} copy-done((f32[1152,1536]{1,0:T(8,128)}, f32[1152,1536]{1,0:T(8,128)S(1)}, u32[]{:S(2)}) %copy-start) | copy-done | bytes 7077912
  160.9 2.3 %fusion.36 = (bf16[32,16,8,128]{3,2,1,0:T(8,128)(2,1)S(1)}, bf16[32,16,8,128]{3,2,1,0:T(8,128)(2,1)S(1)}) fusion(bf16[32,16,9,128]{3,2,1,0:T(8,128)(2,1)} %reshape.152), kind=kLoop, calls=%fused_computation.82 | loop fusion | bytes 4194304 | tf_op jit(solution)/shard_map/slice | solution.py:118
  163.2 5.8 %fusion = f32[32,8,128,16]{2,3,1,0:T(8,128)S(1)} fusion(pred[8,128,128]{2,1,0:T(8,128)(4,1)S(1)} %get-tuple-element.34, bf16[32,128,128]{2,1,0:T(8,128)(2,1)} %copy.23, bf16[32,16,8,128]{3,2,1,0:T(8,128)(2,1)S(1)} %get-tuple-element.14), kind=kOutput, calls=%fused_computation.1 | convolution fusion | flops 138412032 | bytes 4325376 | tf_op jit(solution)/shard_map/gcbj,bgij->gcbi/dot_general | solution.py:120
  169.0 4.5 %add_bitcast_fusion = f32[32,16,8,128]{3,1,2,0:T(8,128)S(1)} fusion(f32[32,8,128,16]{2,3,1,0:T(8,128)S(1)} %fusion, pred[8,128,128]{2,1,0:T(8,128)(4,1)S(1)} %get-tuple-element.33, bf16[32,128,128]{2,1,0:T(8,128)(2,1)S(1)} %copy-done.2, bf16[32,16,8,128]{3,2,1,0:T(8,128)(2,1)S(1)} %get-tuple-element.13), kind=kOutput, calls=%fused_computation.27 | convolution fusion | flops 138936320 | bytes 6422528 | tf_op jit(solution)/shard_map/gcbj,bgij->gcbi/dot_general | solution.py:117
  174.4 1.8 copy.36
  176.2 2.9 %copy.26 = f32[512,1024]{0,1:T(8,128)} copy(f32[512,1024]{1,0:T(8,128)} %bitcast.67) | data formatting | bytes 4194304 | tf_op jit(solution)/shard_map/reshape | solution.py:123
  179.0 2.6 %fusion.17 = bf16[512,1024]{0,1:T(8,128)(2,1)S(1)} fusion(f32[512,1024]{0,1:T(8,128)} %copy.26, f32[1152,1536]{1,0:T(8,128)} %copy-done), kind=kLoop, calls=%fused_computation.26 | loop fusion | flops 1048576 | bytes 5242880 | tf_op jit(solution)/shard_map/convert_element_type | solution.py:124
  183.1 1.7 collective-permute-start.9
  184.9 6.1 %collective-permute-done.8 = bf16[256,512]{1,0:T(8,128)(2,1)S(1)} collective-permute-done((bf16[256,512]{1,0:T(8,128)(2,1)S(1)}, bf16[256,512]{1,0:T(8,128)(2,1)S(1)}, u32[]{:S(2)}, u32[]{:S(2)}) %collective-permute-start.8) | collective-permute-done | bytes 262176 | tf_op jit(solution)/shard_map/ppermute | solution.py:129
  191.0 5.8 %collective-permute-done.9 = bf16[256,512]{1,0:T(8,128)(2,1)S(1)} collective-permute-done((bf16[256,512]{1,0:T(8,128)(2,1)S(1)}, bf16[256,512]{1,0:T(8,128)(2,1)S(1)}, u32[]{:S(2)}, u32[]{:S(2)}) %collective-permute-start.9) | collective-permute-done | bytes 262176 | tf_op jit(solution)/shard_map/ppermute | solution.py:129
  196.8 6.7 %fusion.14 = bf16[256,2048]{1,0:T(8,128)(2,1)} fusion(bf16[2048,2048]{1,0:T(8,128)(2,1)} %pad_maximum_fusion, bf16[256,2048]{1,0:T(8,128)(2,1)S(1)} %copy-done.1, bf16[256,512]{1,0:T(8,128)(2,1)S(1)} %collective-permute-done.9, bf16[256,512]{1,0:T(8,128)(2,1)S(1)} %collective-permute-done.8, bf16[256,512]{1,0:T(8,128)(2,1)S(1)} %collective-permute-done.7, ...), kind=kOutput, calls=%fused_computation.20 | convolution fusion | flops 2153250816 | bytes 11534336 | tf_op jit(solution)/shard_map/dot_general | solution.py:131
  (60 shorter events, 26.0 us)
Async XLA Ops:
  1.9 35.0 %collective-permute-start = (bf16[136,2048]{1,0:T(8,128)(2,1)}, bf16[136,2048]{1,0:T(8,128)(2,1)S(1)}, u32[]{:S(2)}, u32[]{:S(2)}) collective-permute-start(bf16[136,2048]{1,0:T(8,128)(2,1)} %slice.75), channel_id=1, source_target_pairs={{3,7},{7,11},{11,15},{19,23},{23,27},{27,31},{35,39},{39,43},{43,4... | collective-permute-start | bytes 1671176 | tf_op jit(solution)/shard_map/ppermute | solution.py:56
  2.6 42.5 %collective-permute-start.1 = (bf16[136,2048]{1,0:T(8,128)(2,1)}, bf16[136,2048]{1,0:T(8,128)(2,1)}, u32[]{:S(2)}, u32[]{:S(2)}) collective-permute-start(bf16[136,2048]{1,0:T(8,128)(2,1)} %slice.75), channel_id=1, source_target_pairs={{3,6},{7,10},{11,14},{19,22},{23,26},{27,30},{35,38},{39,42},{43,4... | collective-permute-start | bytes 1671176 | tf_op jit(solution)/shard_map/ppermute | solution.py:56
  4.1 41.0 %collective-permute-start.2 = (bf16[136,2048]{1,0:T(8,128)(2,1)}, bf16[136,2048]{1,0:T(8,128)(2,1)}, u32[]{:S(2)}, u32[]{:S(2)}) collective-permute-start(bf16[136,2048]{1,0:T(8,128)(2,1)} %slice.75), channel_id=1, source_target_pairs={{3,5},{7,9},{11,13},{19,21},{23,25},{27,29},{35,37},{39,41},{43,45... | collective-permute-start | bytes 1671176 | tf_op jit(solution)/shard_map/ppermute | solution.py:56
  5.4 39.8 %collective-permute-start.3 = (bf16[136,2048]{1,0:T(8,128)(2,1)}, bf16[136,2048]{1,0:T(8,128)(2,1)}, u32[]{:S(2)}, u32[]{:S(2)}) collective-permute-start(bf16[136,2048]{1,0:T(8,128)(2,1)} %slice.75), channel_id=1, source_target_pairs={{3,4},{7,8},{11,12},{19,20},{23,24},{27,28},{35,36},{39,40},{43,44... | collective-permute-start | bytes 1671176 | tf_op jit(solution)/shard_map/ppermute | solution.py:56
  6.9 33.8 %collective-permute-start.4 = (bf16[256,2048]{1,0:T(8,128)(2,1)}, bf16[256,2048]{1,0:T(8,128)(2,1)S(1)}, u32[]{:S(2)}, u32[]{:S(2)}) collective-permute-start(bf16[256,2048]{1,0:T(8,128)(2,1)} %param.6), channel_id=1, source_target_pairs={{0,2},{1,3},{2,0},{3,1},{4,6},{5,7},{6,4},{7,5},{8,10},{9,11},{10,... | collective-permute-start | bytes 3145736 | tf_op jit(solution)/shard_map/ppermute | solution.py:43
  13.5 6.7 %copy-start.3 = (f32[7,6144]{1,0:T(8,128)S(1)}, f32[7,6144]{1,0:T(8,128)}, u32[]{:S(2)}) copy-start(f32[7,6144]{1,0:T(8,128)} %param.9) | copy-start | bytes 516100
  13.5 7.1 %copy-start.4 = (bf16[128,128]{1,0:T(8,128)(2,1)S(1)}, bf16[128,128]{1,0:T(8,128)(2,1)}, u32[]{:S(2)}) copy-start(bf16[128,128]{1,0:T(8,128)(2,1)} %param.10) | copy-start | bytes 98308
  13.5 7.7 %copy-start.5 = (s32[1,4]{1,0:T(1,128)S(1)}, s32[1,4]{1,0:T(1,128)}, u32[]{:S(2)}) copy-start(s32[1,4]{1,0:T(1,128)} %param.7) | copy-start | bytes 52
  13.5 117.8 %all-to-all-start = ((bf16[16,3,32,2048]{3,2,1,0:T(8,128)(2,1)}), bf16[16,3,32,2048]{3,2,1,0:T(8,128)(2,1)}, u32[]{:S(2)}, u32[]{:S(2)}) async-start(bf16[16,3,32,2048]{3,2,1,0:T(8,128)(2,1)} %stack.2), calls=%async_computation | async-start | bytes 12582912 | tf_op jit(solution)/shard_map/all_to_all | solution.py:68
  32.5 4.4 %copy-start.1 = (bf16[256,2048]{1,0:T(8,128)(2,1)S(1)}, bf16[256,2048]{1,0:T(8,128)(2,1)}, u32[]{:S(2)}) copy-start(bf16[256,2048]{1,0:T(8,128)(2,1)} %param.6) | copy-start | bytes 3145732
  37.0 10.5 %collective-permute-start.6 = (bf16[256,2048]{1,0:T(8,128)(2,1)S(1)}, bf16[256,2048]{1,0:T(8,128)(2,1)S(1)}, u32[]{:S(2)}, u32[]{:S(2)}) collective-permute-start(bf16[256,2048]{1,0:T(8,128)(2,1)S(1)} %copy-done.1), channel_id=1, source_target_pairs={{0,1},{1,0},{2,3},{3,2},{4,5},{5,4},{6,7},{7,6},{8,9},{9,8},{10,11... | collective-permute-start | bytes 3145736 | tf_op jit(solution)/shard_map/ppermute | solution.py:41
  40.6 6.8 %collective-permute-start.5 = (bf16[256,2048]{1,0:T(8,128)(2,1)S(1)}, bf16[256,2048]{1,0:T(8,128)(2,1)S(1)}, u32[]{:S(2)}, u32[]{:S(2)}) collective-permute-start(bf16[256,2048]{1,0:T(8,128)(2,1)S(1)} %collective-permute-done.4), channel_id=1, source_target_pairs={{0,1},{1,0},{2,3},{3,2},{4,5},{5,4},{6,7},{7,6},{8,9},{9,8},{10,11... | collective-permute-start | bytes 3145736 | tf_op jit(solution)/shard_map/ppermute | solution.py:44
  153.2 2.9 %copy-start = (f32[1152,1536]{1,0:T(8,128)}, f32[1152,1536]{1,0:T(8,128)S(1)}, u32[]{:S(2)}) copy-start(f32[1152,1536]{1,0:T(8,128)S(1)} %multiply_add_fusion) | copy-start | bytes 21233668
  163.2 5.8 %copy-start.2 = (bf16[32,128,128]{2,1,0:T(8,128)(2,1)S(1)}, bf16[32,128,128]{2,1,0:T(8,128)(2,1)}, u32[]{:S(2)}) copy-start(bf16[32,128,128]{2,1,0:T(8,128)(2,1)} %copy.20) | copy-start | bytes 3145732
  181.7 3.2 %collective-permute-start.7 = (bf16[256,512]{1,0:T(8,128)(2,1)S(1)}, bf16[256,512]{1,0:T(8,128)(2,1)S(1)}, u32[]{:S(2)}, u32[]{:S(2)}) collective-permute-start(bf16[256,512]{1,0:T(8,128)(2,1)S(1)} %get-tuple-element.18), channel_id=1, source_target_pairs={{0,1},{1,0},{2,3},{3,2},{4,5},{5,4},{6,7},{7,6},{8,9},{9,8},{10,11... | collective-permute-start | bytes 786440 | tf_op jit(solution)/shard_map/ppermute | solution.py:129
  183.1 7.9 %collective-permute-start.8 = (bf16[256,512]{1,0:T(8,128)(2,1)S(1)}, bf16[256,512]{1,0:T(8,128)(2,1)S(1)}, u32[]{:S(2)}, u32[]{:S(2)}) collective-permute-start(bf16[256,512]{1,0:T(8,128)(2,1)S(1)} %get-tuple-element.17), channel_id=1, source_target_pairs={{0,2},{1,3},{2,0},{3,1},{4,6},{5,7},{6,4},{7,5},{8,10},{9,11},{10,... | collective-permute-start | bytes 786440 | tf_op jit(solution)/shard_map/ppermute | solution.py:129
  183.1 13.7 %collective-permute-start.9 = (bf16[256,512]{1,0:T(8,128)(2,1)S(1)}, bf16[256,512]{1,0:T(8,128)(2,1)S(1)}, u32[]{:S(2)}, u32[]{:S(2)}) collective-permute-start(bf16[256,512]{1,0:T(8,128)(2,1)S(1)} %get-tuple-element.16), channel_id=1, source_target_pairs={{0,3},{1,2},{2,1},{3,0},{4,7},{5,6},{6,5},{7,4},{8,11},{9,10},{10,... | collective-permute-start | bytes 786440 | tf_op jit(solution)/shard_map/ppermute | solution.py:129
